TPU v7x, 512 devices: a whole 4x8x8 slice. The times are simulated.
512 devices in a mesh: prompt: 32 (over x, y), sample: 16 (over z, core).
Axes of the slice: x: 4, y: 8, z: 8, core: 2. Of those that a mesh axis runs over, the one named last changes fastest.
Arguments:
- queries: bfloat16 [32, 16, 4, 8192], P('prompt', 'sample'), may hold values from -24 to 24
- new_kv: bfloat16 [32, 16, 4, 2, 1024], P('prompt', 'sample'), may hold values from -24 to 24
- suffix_kv: bfloat16 [32, 16, 256, 2, 1024], P('prompt', 'sample'), may hold values from -24 to 24
- suffix_len: int32 [32, 16], P('prompt', 'sample'), may hold values from 1 to 256, as said below
- prefix_head: bfloat16 [32, 2048, 2, 1024], P('prompt', 'sample'), may hold values from -24 to 24
- prefix_tail: bfloat16 [32, 2048, 2, 1024], P('prompt', 'sample'), may hold values from -24 to 24
- prefix_len: int32 [32], replicated, may hold values from 1024 to 4096, as said below
Outputs:
- attended: bfloat16 [32, 16, 4, 8192], P('prompt', 'sample')
Inputs may be any that keep to these rules, and one draw needn't show every extreme that they name: `suffix_len`: some sample has all 256 slots live and some only one. `prefix_len`: some prompt has all 4096 positions live and some only 1024.
All inputs are finite; a program needn't handle non-finite values.
Results may differ from a plain program's by a relative error of at most 0.001.
Values may be sent and summed in bfloat16 or wider, within the bound.
No kernel may reach another device: no remote copies, remote signals or barrier semaphores. Data moves between devices by JAX's collectives and lax.ppermute only.
A program may use at most 64 MiB of HBM per device.

v0:
```python
import jax
import jax.numpy as jnp
from jax import lax
from jax.sharding import PartitionSpec as P

QH = 64
KVH = 8
HEAD_SIZE = 128
NEG = -1e30


def from_behind(value, axis, steps):
    count = lax.axis_size(axis)
    pairs = [(source, (source + steps) % count) for source in range(count)]
    return lax.ppermute(value, axis, pairs)


def apply_weights(logit_scores, valid_mask, value_matrix, form):
    masked = jnp.where(valid_mask, logit_scores, NEG)
    maxima = jnp.max(masked, axis=-1)
    weights = jnp.where(valid_mask, jnp.exp(masked - maxima[..., None]), 0.0)
    totals = jnp.sum(weights, axis=-1)
    numerator = jnp.einsum(form, weights, value_matrix, precision=lax.Precision.HIGHEST)
    leading = numerator.shape[:2]
    return (
        numerator.reshape(leading + (QH, HEAD_SIZE)),
        maxima.reshape(leading + (QH,)),
        totals.reshape(leading + (QH,)),
    )


def prefix_terms(query_rows, pairs, start, length):
    sample_count, step_count = (query_rows.shape[0], query_rows.shape[1])
    block_len = pairs.shape[0]
    grouped_queries = query_rows.reshape(sample_count, step_count, KVH, QH // KVH, HEAD_SIZE)
    key_matrix = pairs[:, 0].reshape(block_len, KVH, HEAD_SIZE)
    value_matrix = pairs[:, 1].reshape(block_len, KVH, HEAD_SIZE).astype(jnp.float32)
    logit_scores = jnp.einsum(
        "rhlxf,vlf->rhlxv", grouped_queries, key_matrix, preferred_element_type=jnp.float32
    ) * HEAD_SIZE ** (-0.5)
    valid_mask = start + jnp.arange(block_len, dtype=jnp.int32) < length
    return apply_weights(logit_scores, valid_mask, value_matrix, "urpyj,jpi->urpyi")


def suffix_terms(query_rows, cache, fresh, length):
    sample_count, step_count = (query_rows.shape[0], query_rows.shape[1])
    slots = cache.shape[1]
    joined = jnp.concatenate([cache, fresh], axis=1)
    total_len = joined.shape[1]
    grouped_queries = query_rows.reshape(sample_count, step_count, KVH, QH // KVH, HEAD_SIZE)
    key_matrix = joined[:, :, 0].reshape(sample_count, total_len, KVH, HEAD_SIZE)
    value_matrix = (
        joined[:, :, 1].reshape(sample_count, total_len, KVH, HEAD_SIZE).astype(jnp.float32)
    )
    logit_scores = jnp.einsum(
        "stkgd,slkd->stkgl", grouped_queries, key_matrix, preferred_element_type=jnp.float32
    ) * HEAD_SIZE ** (-0.5)
    cache_live = jnp.arange(slots, dtype=jnp.int32)[None, :] < length[:, None]
    steps_live = (
        jnp.arange(step_count, dtype=jnp.int32)[None, :]
        <= jnp.arange(step_count, dtype=jnp.int32)[:, None]
    )
    valid_mask = jnp.concatenate(
        [
            jnp.broadcast_to(cache_live[:, None, :], (sample_count, step_count, slots)),
            steps_live[None],
        ],
        axis=2,
    )
    return apply_weights(
        logit_scores, valid_mask[:, :, None, None, :], value_matrix, "stkgl,slkd->stkgd"
    )


def join(former, latter):
    maxima = jnp.maximum(former[1], latter[1])
    scale_a = jnp.exp(former[1] - maxima)
    scale_b = jnp.exp(latter[1] - maxima)
    return (
        former[0] * scale_a[..., None] + latter[0] * scale_b[..., None],
        maxima,
        former[2] * scale_a + latter[2] * scale_b,
    )


def settle(stacked):
    maxima = jnp.max(stacked[1], axis=0)
    factors = jnp.exp(stacked[1] - maxima[None])
    return (
        jnp.sum(stacked[0] * factors[..., None], axis=0),
        maxima,
        jnp.sum(stacked[2] * factors, axis=0),
    )


def spread(partial_sums):
    return (
        lax.all_to_all(partial_sums[0][None], "sample", split_axis=1, concat_axis=0, tiled=True),
        lax.all_to_all(partial_sums[1][None], "sample", split_axis=1, concat_axis=0, tiled=True),
        lax.all_to_all(partial_sums[2][None], "sample", split_axis=1, concat_axis=0, tiled=True),
    )


def per_device(queries, new_kv, suffix_kv, suffix_len, prefix_head, prefix_tail, prefix_len):
    sample_count = lax.axis_size("sample")
    prompt_row = lax.axis_index("prompt")
    sample_slot = lax.axis_index("sample")
    block_len = prefix_head.shape[1]
    half_len = block_len * sample_count
    own_length = prefix_len[prompt_row]
    local_rows = queries[0]
    every_rows = lax.all_gather(queries, "sample", axis=1, tiled=True)[0]
    near_part = suffix_terms(local_rows, suffix_kv[0], new_kv[0], suffix_len[0])
    moved = from_behind(prefix_tail, "prompt", -1)
    own_part = prefix_terms(every_rows, prefix_head[0], sample_slot * block_len, own_length)
    tail_part = prefix_terms(every_rows, moved[0], half_len + sample_slot * block_len, own_length)
    result = join(settle(spread(join(own_part, tail_part))), near_part)
    attended = (result[0] / result[2][..., None]).astype(jnp.bfloat16)
    return attended.reshape(queries.shape)


def solution(mesh):
    in_specs = (
        P("prompt", "sample", None, None),
        P("prompt", "sample", None, None, None),
        P("prompt", "sample", None, None, None),
        P("prompt", "sample"),
        P("prompt", "sample", None, None),
        P("prompt", "sample", None, None),
        P(),
    )
    out_specs = P("prompt", "sample", None, None)
    return jax.shard_map(
        per_device, mesh=mesh, in_specs=in_specs, out_specs=out_specs, check_vma=False
    )
```

profile of v0, /device:TPU:1, one launch (start us, length us, event | category | flops | bytes accessed | tf_op | source)
XLA Modules:
  0.0 154.0 jit_solution(10899200841303403284)
XLA Ops:
  6.5 0.0 copy-start.3
  6.5 0.0 all-gather.2.cloned.1.call-start
  6.5 0.7 all-gather.2.cloned.1.call-update
  7.3 1.4 copy.107
  8.6 8.1 %collective-permute-start = (bf16[1,128,2,1024]{1,3,2,0:T(8,128)(2,1)S(1)}, bf16[1,128,2,1024]{1,3,2,0:T(8,128)(2,1)S(1)}, u32[]{:S(2)}, u32[]{:S(2)}) collective-permute-start(bf16[1,128,2,1024]{1,3,2,0:T(8,128)(2,1)S(1)} %copy.107), channel_id=1, source_target_pairs={{0,496},{16,0},{32,16},{48,32},{64,48},{80,64},{96,80},{112,96},{1... | collective-permute-start | bytes 1572872 | tf_op jit(solution)/shard_map/ppermute | solution.py:15
  16.8 1.4 copy.98
  18.2 0.0 copy-done.3
  18.2 0.6 dynamic_slice.3
  18.8 0.7 add_compare_fusion.1
  19.4 0.7 add_compare_fusion
  20.1 7.2 %collective-permute-done = bf16[1,128,2,1024]{1,3,2,0:T(8,128)(2,1)S(1)} collective-permute-done((bf16[1,128,2,1024]{1,3,2,0:T(8,128)(2,1)S(1)}, bf16[1,128,2,1024]{1,3,2,0:T(8,128)(2,1)S(1)}, u32[]{:S(2)}, u32[]{:S(2)}) %collective-permute-start) | collective-permute-done | bytes 524320 | tf_op jit(solution)/shard_map/ppermute | solution.py:15
  27.4 30.0 %all-gather.2.cloned.1.call-done = bf16[1,16,4,8192]{3,2,0,1:T(4,128)(2,1)} async-done(((bf16[1,1,4,8192]{3,2,0,1:T(4,128)(2,1)}), bf16[1,16,4,8192]{3,2,0,1:T(4,128)(2,1)}) %all-gather.2.cloned.1.call-update) | async-done | bytes 1048592 | tf_op jit(solution)/shard_map/all_gather | solution.py:112
  57.4 2.1 %reshape.433 = bf16[16,4,8,8,128]{4,3,2,1,0:T(8,128)(2,1)S(1)} reshape(bf16[1,16,4,8192]{3,2,0,1:T(4,128)(2,1)} %all-gather.2.cloned.1.call-done) | data formatting | bytes 2097152 | tf_op jit(solution)/shard_map/reshape;squeeze | solution.py:35
  59.5 1.0 bitcast_reduce_fusion
  60.6 1.0 bitcast_reduce_fusion.1
  61.6 3.3 %fusion.47 = (f32[16,4,8,8]{0,3,1,2:T(8,128)S(1)}, f32[16,4,8,8,128]{4,0,3,1,2:T(8,128)}, f32[16,4,8,8]{0,3,1,2:T(8,128)S(1)}, f32[16,4,8,8,128]{4,0,3,1,2:T(8,128)}) fusion(f32[16,4,8,8]{0,3,1,2:T(8,128)S(1)} %get-tuple-element.26, f32[8,128,16,4,8]{1,2,4,3,0:T(8,128)S(1)} %get-tuple-element.27, pred[128]{0:T(512)(128)(4,1)S(1)} %add_compare_fusion.1, ...), kind=kLoop, calls=%fused_computation.79 | loop fusion | flops 5234688 | bytes 8454400 | tf_op jit(solution)/shard_map/reduce_sum | solution.py:22
  64.9 0.1 fusion.31
  64.9 0.1 copy.123
  65.0 0.7 reshape.437
  65.7 4.5 %all-to-all-start.1 = ((f32[16,1,256]{2,1,0:T(1,128)}), f32[16,1,256]{2,1,0:T(1,128)S(1)}, u32[]{:S(2)}, u32[]{:S(2)}) async-start(f32[16,1,256]{2,1,0:T(1,128)} %reshape.437), calls=%async_computation.1 | async-start | bytes 32768 | tf_op jit(solution)/shard_map/all_to_all | solution.py:99
  70.2 0.1 copy.112
  70.3 0.1 copy.113
  70.4 0.0 copy-start
  70.4 3.4 %fusion.11 = f32[16,4,8,8,128]{4,3,1,0,2:T(8,128)S(1)} fusion(bf16[128,8,128,1,1]{0,2,4,3,1:T(8,128)(2,1)S(1)} %bitcast.166, f32[16,4,8,8,128]{4,0,3,1,2:T(8,128)} %get-tuple-element.11), kind=kOutput, calls=%fused_computation.20 | convolution fusion | flops 805306368 | bytes 4456448 | tf_op jit(solution)/shard_map/urpyj,jpi->urpyi/dot_general | solution.py:23
  73.8 0.0 copy-done
  73.8 3.1 %fusion.14 = f32[16,4,8,8,128]{4,3,1,0,2:T(8,128)} fusion(bf16[128,8,128,1,1]{0,2,4,3,1:T(8,128)(2,1)S(1)} %bitcast.167, f32[16,4,8,8,128]{4,0,3,1,2:T(8,128)S(1)} %copy-done), kind=kOutput, calls=%fused_computation.21 | convolution fusion | flops 805306368 | bytes 4456448 | tf_op jit(solution)/shard_map/urpyj,jpi->urpyi/dot_general | solution.py:23
  76.9 0.1 copy.131
  77.0 0.7 reshape.439
  77.7 0.0 all-to-all-done.1
  77.7 7.2 %all-to-all-start.2 = ((f32[16,1,256]{2,1,0:T(1,128)}), f32[16,1,256]{2,1,0:T(1,128)S(1)}, u32[]{:S(2)}, u32[]{:S(2)}) async-start(f32[16,1,256]{2,1,0:T(1,128)} %reshape.439), calls=%async_computation.2 | async-start | bytes 32768 | tf_op jit(solution)/shard_map/all_to_all | solution.py:100
  84.9 3.4 %fusion.2 = f32[1,16,4,64,128]{4,3,2,0,1:T(8,128)} fusion(f32[16,4,8,8,128]{4,3,1,0,2:T(8,128)} %fusion.14, f32[16,4,8,8,128]{4,3,1,0,2:T(8,128)S(1)} %fusion.11, f32[16,4,64]{2,1,0:T(4,128)S(1)} %copy.119, f32[16,4,64]{2,1,0:T(4,128)S(1)} %copy.114), kind=kLoop, calls=%fused_computation.4 | loop fusion | flops 1572864 | bytes 6324224 | tf_op jit(solution)/shard_map/add | solution.py:80
  88.4 0.0 copy-start.2
  88.4 3.9 %all-to-all-done.2 = f32[16,1,256]{2,1,0:T(1,128)S(1)} async-done(((f32[16,1,256]{2,1,0:T(1,128)}), f32[16,1,256]{2,1,0:T(1,128)S(1)}, u32[]{:S(2)}, u32[]{:S(2)}) %all-to-all-start.2) | async-done | bytes 16416 | tf_op jit(solution)/shard_map/all_to_all | solution.py:100
  92.3 3.9 %all-to-all-start = ((f32[1,16,4,64,128]{4,3,2,0,1:T(8,128)}), f32[1,16,4,64,128]{4,3,2,0,1:T(8,128)S(1)}, u32[]{:S(2)}, u32[]{:S(2)}) async-start(f32[1,16,4,64,128]{4,3,2,0,1:T(8,128)} %fusion.2), calls=%async_computation | async-start | bytes 4194304 | tf_op jit(solution)/shard_map/all_to_all | solution.py:98
  96.8 0.0 copy-done.2
  96.8 0.0 copy-start.1
  96.8 12.8 %fusion.19 = (bf16[260,1024]{1,0:T(8,128)(2,1)S(1)}, bf16[260,1024]{1,0:T(8,128)(2,1)S(1)}) fusion(bf16[1,4,2,1024]{3,2,1,0:T(2,128)(2,1)S(1)} %bitcast.181, bf16[1,256,2,1024]{3,2,1,0:T(2,128)(2,1)} %bitcast.165), kind=kLoop, calls=%fused_computation.28 | loop fusion | flops 2129920 | bytes 2129920 | tf_op jit(solution)/shard_map/slice | solution.py:53
  109.6 0.1 copy.155
  109.8 0.0 copy-done.1
  109.8 0.4 fusion.53
  110.2 0.2 fusion.27
  110.5 0.1 reshape.426
  110.6 0.1 reshape.420
  110.6 0.1 copy.157
  110.8 0.5 convolution_bitcast_fusion
  111.4 0.5 broadcast.97
  111.9 0.7 reduce.10
  112.6 0.1 reshape.438
  112.6 0.7 reduce.11
  113.3 0.1 reshape.440
  113.5 31.7 %all-to-all-done = f32[1,16,4,64,128]{4,3,2,0,1:T(8,128)S(1)} async-done(((f32[1,16,4,64,128]{4,3,2,0,1:T(8,128)}), f32[1,16,4,64,128]{4,3,2,0,1:T(8,128)S(1)}, u32[]{:S(2)}, u32[]{:S(2)}) %all-to-all-start) | async-done | bytes 2097184 | tf_op jit(solution)/shard_map/all_to_all | solution.py:98
  145.2 0.7 fusion
  145.9 0.1 broadcast_multiply_fusion
  146.0 0.1 mul.174
  146.1 0.1 div.19
  146.2 0.2 fusion.34
  146.4 0.7 copy.133
  (20 shorter events, 0.4 us)
Async XLA Ops:
  6.5 11.6 %copy-start.3 = (s32[32]{0:T(128)S(1)}, s32[32]{0:T(128)}, u32[]{:S(2)}) copy-start(s32[32]{0:T(128)} %param.13) | copy-start | bytes 388
  6.5 50.8 %all-gather.2.cloned.1.call-start = ((), (), s32[]{:S(2)}) async-start(), calls=%async_computation.3 | async-start | bytes 1114112 | tf_op jit(solution)/shard_map/all_gather | solution.py:112
  8.6 18.7 %collective-permute-start = (bf16[1,128,2,1024]{1,3,2,0:T(8,128)(2,1)S(1)}, bf16[1,128,2,1024]{1,3,2,0:T(8,128)(2,1)S(1)}, u32[]{:S(2)}, u32[]{:S(2)}) collective-permute-start(bf16[1,128,2,1024]{1,3,2,0:T(8,128)(2,1)S(1)} %copy.107), channel_id=1, source_target_pairs={{0,496},{16,0},{32,16},{48,32},{64,48},{80,64},{96,80},{112,96},{1... | collective-permute-start | bytes 1572872 | tf_op jit(solution)/shard_map/ppermute | solution.py:15
  65.7 12.0 %all-to-all-start.1 = ((f32[16,1,256]{2,1,0:T(1,128)}), f32[16,1,256]{2,1,0:T(1,128)S(1)}, u32[]{:S(2)}, u32[]{:S(2)}) async-start(f32[16,1,256]{2,1,0:T(1,128)} %reshape.437), calls=%async_computation.1 | async-start | bytes 32768 | tf_op jit(solution)/shard_map/all_to_all | solution.py:99
  70.4 3.4 %copy-start = (f32[16,4,8,8,128]{4,0,3,1,2:T(8,128)S(1)}, f32[16,4,8,8,128]{4,0,3,1,2:T(8,128)}, u32[]{:S(2)}) copy-start(f32[16,4,8,8,128]{4,0,3,1,2:T(8,128)} %get-tuple-element.29) | copy-start | bytes 6291460
  77.7 14.6 %all-to-all-start.2 = ((f32[16,1,256]{2,1,0:T(1,128)}), f32[16,1,256]{2,1,0:T(1,128)S(1)}, u32[]{:S(2)}, u32[]{:S(2)}) async-start(f32[16,1,256]{2,1,0:T(1,128)} %reshape.439), calls=%async_computation.2 | async-start | bytes 32768 | tf_op jit(solution)/shard_map/all_to_all | solution.py:100
  88.4 8.4 %copy-start.2 = (bf16[1,1,4,2,1024]{4,3,2,1,0:T(2,128)(2,1)S(1)}, bf16[1,1,4,2,1024]{4,3,2,1,0:T(2,128)(2,1)}, u32[]{:S(2)}) copy-start(bf16[1,1,4,2,1024]{4,3,2,1,0:T(2,128)(2,1)} %param.8) | copy-start | bytes 49156
  92.3 52.9 %all-to-all-start = ((f32[1,16,4,64,128]{4,3,2,0,1:T(8,128)}), f32[1,16,4,64,128]{4,3,2,0,1:T(8,128)S(1)}, u32[]{:S(2)}, u32[]{:S(2)}) async-start(f32[1,16,4,64,128]{4,3,2,0,1:T(8,128)} %fusion.2), calls=%async_computation | async-start | bytes 4194304 | tf_op jit(solution)/shard_map/all_to_all | solution.py:98
  96.8 13.0 %copy-start.1 = (bf16[1,1,4,8192]{3,2,1,0:T(4,128)(2,1)S(1)}, bf16[1,1,4,8192]{3,2,1,0:T(4,128)(2,1)}, u32[]{:S(2)}) copy-start(bf16[1,1,4,8192]{3,2,1,0:T(4,128)(2,1)} %param.7) | copy-start | bytes 196612
Sparse Core Ops, SparseCore 0:
  9.5 47.8 all-gather.1
where the time goes:
time: 154 us
  waiting for transfers between devices  73.5 us (48%)
  starting transfers between devices  23.7 us (15%)
  other arithmetic  23.6 us (15%)
  between operations  14.4 us (9%)
  matrix products  9.42 us (6%)
  local copies, waits for them, and re-layouts  9.41 us (6%)
    all_to_all x1, waiting for transfers between devices, spread(): lax.all_to_all(partial_sums[0][None], 'sample', split_axis=1, concat_axis...  31.7 us
    all_gather x1, waiting for transfers between devices, per_device(): every_rows = lax.all_gather(queries, 'sample', axis=1, tiled=True)[0]  30 us
    slice x1, other arithmetic, suffix_terms(): joined[:, :, 1].reshape(sample_count, total_len, KVH, HEAD_SIZE)  12.8 us
    ppermute x1, starting transfers between devices, from_behind(): return lax.ppermute(value, axis, pairs)  8.12 us
    all_to_all x1, starting transfers between devices, spread(): lax.all_to_all(partial_sums[2][None], 'sample', split_axis=1, concat_axis...  7.22 us
    ppermute x1, waiting for transfers between devices, from_behind(): return lax.ppermute(value, axis, pairs)  7.22 us
    dot_general x3, matrix products, apply_weights(): jnp.einsum(form, weights, value_matrix, precision=lax.Precision.HIGHEST)  7.01 us
    unnamed x16, local copies, waits for them, and re-layouts  4.55 us
  transfers between devices with their start and end apart: 5, of which 4 were waited for; matrix products, arithmetic and copies ran while one was open for 21% of the time, Pallas kernels for 0%

commit v1 on v0

--- a/solution.py
+++ b/solution.py
@@ -109,7 +109,37 @@
     half_len = block_len * sample_count
     own_length = prefix_len[prompt_row]
     local_rows = queries[0]
-    every_rows = lax.all_gather(queries, "sample", axis=1, tiled=True)[0]
+
+    def _number_flows(here_x, k_dim=1):
+        back, r_now, x_now = (
+            lax.axis_size("sample"),
+            lax.axis_index("sample"),
+            here_x.shape[k_dim],
+        )
+        arrivals = [ii * back if dev == k_dim else ii for dev, ii in enumerate(here_x.shape)]
+        seen_now = lax.dynamic_update_slice_in_dim(
+            jnp.zeros(arrivals, here_x.dtype), here_x, r_now * x_now, axis=k_dim
+        )
+        g_now = local_part = here_x
+        for d in range(1, back // 2 + 1):
+            g_now = lax.ppermute(
+                g_now, "sample", list(map(lambda dev: (dev, (dev + 1) % back), range(back)))
+            )
+            seen_now = lax.dynamic_update_slice_in_dim(
+                seen_now, g_now, (r_now - d) % back * x_now, axis=k_dim
+            )
+            if 2 * d < back:
+                local_part = lax.ppermute(
+                    local_part,
+                    "sample",
+                    perm=list(map(lambda dev: (dev, (dev - 1) % back), range(back))),
+                )
+                seen_now = lax.dynamic_update_slice_in_dim(
+                    seen_now, local_part, (r_now + d) % back * x_now, axis=k_dim
+                )
+        return seen_now
+
+    every_rows = _number_flows(queries)[0]
     near_part = suffix_terms(local_rows, suffix_kv[0], new_kv[0], suffix_len[0])
     moved = from_behind(prefix_tail, "prompt", -1)
     own_part = prefix_terms(every_rows, prefix_head[0], sample_slot * block_len, own_length)

time: 154 us -> 182 us (1.18)
  local copies, waits for them, and re-layouts: 9.41 us -> 47.5 us
  waiting for transfers between devices: 73.5 us -> 40.8 us
  starting transfers between devices: 23.7 us -> 56 us
  between operations: 14.4 us -> 1.58 us
    dynamic_update_slice x0 -> x16, local copies, waits for them, and re-layouts: none -> 32 us  [the longest x8 16 us: _number_flows(): lax.dynamic_update_slice_in_dim(seen_now, g_now, (r_now - d) % back * x_n...]
    ppermute x0 -> x15, starting transfers between devices: none -> 30.3 us  [the longest x7 26.8 us: _number_flows(): lax.ppermute(local_part, 'sample', perm=list(map(lambda dev: (dev, (dev -...]
    all_gather x1 -> x0, waiting for transfers between devices: 30 us -> none  [per_device(): every_rows = lax.all_gather(queries, 'sample', axis=1, tiled=True)[0]]
    ppermute x1, waiting for transfers between devices: 7.22 us -> 0.01 us  [from_behind(): return lax.ppermute(value, axis, pairs)]
    ppermute x0 -> x15, waiting for transfers between devices: none -> 4.56 us  [the longest x8 3.91 us: _number_flows(): lax.ppermute(g_now, 'sample', list(map(lambda dev: (dev, (dev + 1) % back...]
    all_to_all x1, starting transfers between devices: 4.46 us -> 7.93 us  [spread(): lax.all_to_all(partial_sums[1][None], 'sample', split_axis=1, concat_axis...]
    slice x2, local copies, waits for them, and re-layouts: 0.07 us -> 2.6 us  [prefix_terms(): pairs[:, 1].reshape(block_len, KVH, HEAD_SIZE).astype(jnp.float32)]
    dot_general x2, matrix products: 2.02 us -> 4.53 us  [prefix_terms(): jnp.einsum('rhlxf,vlf->rhlxv', grouped_queries, key_matrix, preferred_ele...]
  transfers between devices with their start and end apart: 5 -> 19, of which waited for: 4 -> 12; matrix products, arithmetic and copies ran while one was open for 21% -> 40% of each run, Pallas kernels for 0% -> 0%
where the time goes in v1:
time: 182 us; the launch traced here: 181 us
  starting transfers between devices  56 us (31%)
  local copies, waits for them, and re-layouts  47.5 us (26%)
  waiting for transfers between devices  40.8 us (22%)
  other arithmetic  24.4 us (13%)
  matrix products  10.9 us (6%)
    all_to_all x1, waiting for transfers between devices, spread(): lax.all_to_all(partial_sums[0][None], 'sample', split_axis=1, concat_axis...  31.6 us
    ppermute x7, starting transfers between devices, _number_flows(): lax.ppermute(local_part, 'sample', perm=list(map(lambda dev: (dev, (dev -...  26.8 us
    dynamic_update_slice x8, local copies, waits for them, and re-layouts, _number_flows(): lax.dynamic_update_slice_in_dim(seen_now, g_now, (r_now - d) % back * x_n...  16 us
    dynamic_update_slice x7, local copies, waits for them, and re-layouts, _number_flows(): lax.dynamic_update_slice_in_dim(seen_now, local_part, (r_now + d) % back...  14 us
    slice x1, other arithmetic, suffix_terms(): joined[:, :, 1].reshape(sample_count, total_len, KVH, HEAD_SIZE)  12.8 us
    all_to_all x1, starting transfers between devices, spread(): lax.all_to_all(partial_sums[1][None], 'sample', split_axis=1, concat_axis...  7.93 us
    ppermute x1, starting transfers between devices, from_behind(): return lax.ppermute(value, axis, pairs)  7.28 us
    all_to_all x1, starting transfers between devices, spread(): lax.all_to_all(partial_sums[2][None], 'sample', split_axis=1, concat_axis...  6.6 us
  transfers between devices with their start and end apart: 19, of which 12 were waited for; matrix products, arithmetic and copies ran while one was open for 40% of the time, Pallas kernels for 0%

profile of v1, /device:TPU:1, one launch (start us, length us, event | category | flops | bytes accessed | tf_op | source)
XLA Modules:
  0.0 181.2 jit_solution(17467634662229346618)
XLA Ops:
  0.0 3.5 %collective-permute-start = (bf16[1,1,4,8192]{3,2,1,0:T(4,128)(2,1)}, bf16[1,1,4,8192]{3,2,1,0:T(4,128)(2,1)S(1)}, u32[]{:S(2)}, u32[]{:S(2)}) collective-permute-start(bf16[1,1,4,8192]{3,2,1,0:T(4,128)(2,1)} %param.7), channel_id=1, source_target_pairs={{0,1},{1,2},{2,3},{3,4},{4,5},{5,6},{6,7},{7,8},{8,9},{9,10},{10,1... | collective-permute-start | bytes 196616 | tf_op jit(solution)/shard_map/ppermute | solution.py:125
  3.5 3.4 %collective-permute-start.1 = (bf16[1,1,4,8192]{3,2,1,0:T(4,128)(2,1)}, bf16[1,1,4,8192]{3,2,1,0:T(4,128)(2,1)S(1)}, u32[]{:S(2)}, u32[]{:S(2)}) collective-permute-start(bf16[1,1,4,8192]{3,2,1,0:T(4,128)(2,1)} %param.7), channel_id=1, source_target_pairs={{0,15},{1,0},{2,1},{3,2},{4,3},{5,4},{6,5},{7,6},{8,7},{9,8},{10,9... | collective-permute-start | bytes 196616 | tf_op jit(solution)/shard_map/ppermute | solution.py:132
  6.9 1.0 collective-permute-done
  8.0 4.2 %collective-permute-start.3 = (bf16[1,1,4,8192]{3,2,1,0:T(4,128)(2,1)S(1)}, bf16[1,1,4,8192]{3,2,1,0:T(4,128)(2,1)S(1)}, u32[]{:S(2)}, u32[]{:S(2)}) collective-permute-start(bf16[1,1,4,8192]{3,2,1,0:T(4,128)(2,1)S(1)} %collective-permute-done.1), channel_id=1, source_target_pairs={{0,15},{1,0},{2,1},{3,2},{4,3},{5,4},{6,5},{7,6},{8,7},{9,8},{10,9... | collective-permute-start | bytes 196616 | tf_op jit(solution)/shard_map/ppermute | solution.py:132
  12.2 0.7 collective-permute-done.2
  13.1 4.0 %collective-permute-start.5 = (bf16[1,1,4,8192]{3,2,1,0:T(4,128)(2,1)S(1)}, bf16[1,1,4,8192]{3,2,1,0:T(4,128)(2,1)S(1)}, u32[]{:S(2)}, u32[]{:S(2)}) collective-permute-start(bf16[1,1,4,8192]{3,2,1,0:T(4,128)(2,1)S(1)} %collective-permute-done.3), channel_id=1, source_target_pairs={{0,15},{1,0},{2,1},{3,2},{4,3},{5,4},{6,5},{7,6},{8,7},{9,8},{10,9... | collective-permute-start | bytes 196616 | tf_op jit(solution)/shard_map/ppermute | solution.py:132
  17.1 0.7 collective-permute-done.4
  18.0 4.0 %collective-permute-start.7 = (bf16[1,1,4,8192]{3,2,1,0:T(4,128)(2,1)S(1)}, bf16[1,1,4,8192]{3,2,1,0:T(4,128)(2,1)S(1)}, u32[]{:S(2)}, u32[]{:S(2)}) collective-permute-start(bf16[1,1,4,8192]{3,2,1,0:T(4,128)(2,1)S(1)} %collective-permute-done.5), channel_id=1, source_target_pairs={{0,15},{1,0},{2,1},{3,2},{4,3},{5,4},{6,5},{7,6},{8,7},{9,8},{10,9... | collective-permute-start | bytes 196616 | tf_op jit(solution)/shard_map/ppermute | solution.py:132
  22.0 0.7 collective-permute-done.6
  22.9 4.0 %collective-permute-start.9 = (bf16[1,1,4,8192]{3,2,1,0:T(4,128)(2,1)S(1)}, bf16[1,1,4,8192]{3,2,1,0:T(4,128)(2,1)S(1)}, u32[]{:S(2)}, u32[]{:S(2)}) collective-permute-start(bf16[1,1,4,8192]{3,2,1,0:T(4,128)(2,1)S(1)} %collective-permute-done.7), channel_id=1, source_target_pairs={{0,15},{1,0},{2,1},{3,2},{4,3},{5,4},{6,5},{7,6},{8,7},{9,8},{10,9... | collective-permute-start | bytes 196616 | tf_op jit(solution)/shard_map/ppermute | solution.py:132
  26.9 0.7 collective-permute-done.8
  27.7 2.0 %copy.155 = bf16[1,128,2,1024]{1,3,2,0:T(8,128)(2,1)} copy(bf16[1,128,2,1024]{3,2,1,0:T(2,128)(2,1)} %param.12) | data formatting | bytes 1048576 | tf_op args[5]
  29.7 7.3 %collective-permute-start.15 = (bf16[1,128,2,1024]{1,3,2,0:T(8,128)(2,1)}, bf16[1,128,2,1024]{1,3,2,0:T(8,128)(2,1)}, u32[]{:S(2)}, u32[]{:S(2)}) collective-permute-start(bf16[1,128,2,1024]{1,3,2,0:T(8,128)(2,1)} %copy.155), channel_id=1, source_target_pairs={{0,496},{16,0},{32,16},{48,32},{64,48},{80,64},{96,80},{112,96},{1... | collective-permute-start | bytes 1572872 | tf_op jit(solution)/shard_map/ppermute | solution.py:15
  37.0 1.4 copy.149
  38.4 4.4 %collective-permute-start.11 = (bf16[1,1,4,8192]{3,2,1,0:T(4,128)(2,1)S(1)}, bf16[1,1,4,8192]{3,2,1,0:T(4,128)(2,1)S(1)}, u32[]{:S(2)}, u32[]{:S(2)}) collective-permute-start(bf16[1,1,4,8192]{3,2,1,0:T(4,128)(2,1)S(1)} %collective-permute-done.9), channel_id=1, source_target_pairs={{0,15},{1,0},{2,1},{3,2},{4,3},{5,4},{6,5},{7,6},{8,7},{9,8},{10,9... | collective-permute-start | bytes 196616 | tf_op jit(solution)/shard_map/ppermute | solution.py:132
  42.8 0.8 fusion.59
  44.1 0.6 dynamic_slice.3
  44.7 2.0 %dynamic_update_slice.48 = bf16[1,16,4,8192]{3,1,2,0:T(8,128)(2,1)S(1)} dynamic-update-slice(bf16[1,16,4,8192]{3,1,2,0:T(8,128)(2,1)S(1)} %broadcast_in_dim.71, bf16[1,1,4,8192]{3,1,2,0:T(2,128)(2,1)S(1)} %copy.133, s32[]{:T(128)} %constant.102.clone.1, s32[]{:T(128)S(6)} %select_n.141, s32[]{:T(128)} %constant.102.clone.1, s32[]{:T(128)} %constant.102.clone.1) | dynamic-update-slice | bytes 131076 | tf_op jit(solution)/shard_map/dynamic_update_slice | solution.py:120
  46.7 2.7 %collective-permute-start.13 = (bf16[1,1,4,8192]{3,2,1,0:T(4,128)(2,1)S(1)}, bf16[1,1,4,8192]{3,2,1,0:T(4,128)(2,1)S(1)}, u32[]{:S(2)}, u32[]{:S(2)}) collective-permute-start(bf16[1,1,4,8192]{3,2,1,0:T(4,128)(2,1)S(1)} %collective-permute-done.11), channel_id=1, source_target_pairs={{0,15},{1,0},{2,1},{3,2},{4,3},{5,4},{6,5},{7,6},{8,7},{9,8},{10,9... | collective-permute-start | bytes 196616 | tf_op jit(solution)/shard_map/ppermute | solution.py:132
  49.4 0.7 add_compare_fusion
  50.2 2.0 %dynamic_update_slice.49 = bf16[1,16,4,8192]{3,1,2,0:T(8,128)(2,1)S(1)} dynamic-update-slice(bf16[1,16,4,8192]{3,1,2,0:T(8,128)(2,1)S(1)} %dynamic_update_slice.48, bf16[1,1,4,8192]{3,1,2,0:T(2,128)(2,1)S(1)} %copy.134, s32[]{:T(128)} %constant.102.clone.1, s32[]{:T(128)S(6)} %select_n.143, s32[]{:T(128)} %constant.102.clone.1, s32[]{:T(128)} %constant.102.clone.1) | dynamic-update-slice | bytes 131076 | tf_op jit(solution)/shard_map/dynamic_update_slice | solution.py:128
  52.3 2.0 %dynamic_update_slice.50 = bf16[1,16,4,8192]{3,1,2,0:T(8,128)(2,1)S(1)} dynamic-update-slice(bf16[1,16,4,8192]{3,1,2,0:T(8,128)(2,1)S(1)} %dynamic_update_slice.49, bf16[1,1,4,8192]{3,1,2,0:T(2,128)(2,1)S(1)} %copy.135, s32[]{:T(128)} %constant.102.clone.1, s32[]{:T(128)S(6)} %select_n.145, s32[]{:T(128)} %constant.102.clone.1, s32[]{:T(128)} %constant.102.clone.1) | dynamic-update-slice | bytes 131076 | tf_op jit(solution)/shard_map/dynamic_update_slice | solution.py:137
  54.4 2.0 %dynamic_update_slice.51 = bf16[1,16,4,8192]{3,1,2,0:T(8,128)(2,1)S(1)} dynamic-update-slice(bf16[1,16,4,8192]{3,1,2,0:T(8,128)(2,1)S(1)} %dynamic_update_slice.50, bf16[1,1,4,8192]{3,1,2,0:T(2,128)(2,1)S(1)} %copy.136, s32[]{:T(128)} %constant.102.clone.1, s32[]{:T(128)S(6)} %select_n.147, s32[]{:T(128)} %constant.102.clone.1, s32[]{:T(128)} %constant.102.clone.1) | dynamic-update-slice | bytes 131076 | tf_op jit(solution)/shard_map/dynamic_update_slice | solution.py:128
  56.6 2.0 %dynamic_update_slice.52 = bf16[1,16,4,8192]{3,1,2,0:T(8,128)(2,1)S(1)} dynamic-update-slice(bf16[1,16,4,8192]{3,1,2,0:T(8,128)(2,1)S(1)} %dynamic_update_slice.51, bf16[1,1,4,8192]{3,1,2,0:T(2,128)(2,1)S(1)} %copy.137, s32[]{:T(128)} %constant.102.clone.1, s32[]{:T(128)S(6)} %select_n.149, s32[]{:T(128)} %constant.102.clone.1, s32[]{:T(128)} %constant.102.clone.1) | dynamic-update-slice | bytes 131076 | tf_op jit(solution)/shard_map/dynamic_update_slice | solution.py:137
  58.7 2.0 %dynamic_update_slice.53 = bf16[1,16,4,8192]{3,1,2,0:T(8,128)(2,1)S(1)} dynamic-update-slice(bf16[1,16,4,8192]{3,1,2,0:T(8,128)(2,1)S(1)} %dynamic_update_slice.52, bf16[1,1,4,8192]{3,1,2,0:T(2,128)(2,1)S(1)} %copy.138, s32[]{:T(128)} %constant.102.clone.1, s32[]{:T(128)S(6)} %select_n.151, s32[]{:T(128)} %constant.102.clone.1, s32[]{:T(128)} %constant.102.clone.1) | dynamic-update-slice | bytes 131076 | tf_op jit(solution)/shard_map/dynamic_update_slice | solution.py:128
  60.8 2.0 %dynamic_update_slice.54 = bf16[1,16,4,8192]{3,1,2,0:T(8,128)(2,1)S(1)} dynamic-update-slice(bf16[1,16,4,8192]{3,1,2,0:T(8,128)(2,1)S(1)} %dynamic_update_slice.53, bf16[1,1,4,8192]{3,1,2,0:T(2,128)(2,1)S(1)} %copy.139, s32[]{:T(128)} %constant.102.clone.1, s32[]{:T(128)S(6)} %select_n.153, s32[]{:T(128)} %constant.102.clone.1, s32[]{:T(128)} %constant.102.clone.1) | dynamic-update-slice | bytes 131076 | tf_op jit(solution)/shard_map/dynamic_update_slice | solution.py:137
  62.9 2.0 %dynamic_update_slice.55 = bf16[1,16,4,8192]{3,1,2,0:T(8,128)(2,1)S(1)} dynamic-update-slice(bf16[1,16,4,8192]{3,1,2,0:T(8,128)(2,1)S(1)} %dynamic_update_slice.54, bf16[1,1,4,8192]{3,1,2,0:T(2,128)(2,1)S(1)} %copy.140, s32[]{:T(128)} %constant.102.clone.1, s32[]{:T(128)S(6)} %select_n.155, s32[]{:T(128)} %constant.102.clone.1, s32[]{:T(128)} %constant.102.clone.1) | dynamic-update-slice | bytes 131076 | tf_op jit(solution)/shard_map/dynamic_update_slice | solution.py:128
  65.0 2.0 %dynamic_update_slice.56 = bf16[1,16,4,8192]{3,1,2,0:T(8,128)(2,1)S(1)} dynamic-update-slice(bf16[1,16,4,8192]{3,1,2,0:T(8,128)(2,1)S(1)} %dynamic_update_slice.55, bf16[1,1,4,8192]{3,1,2,0:T(2,128)(2,1)S(1)} %copy.141, s32[]{:T(128)} %constant.102.clone.1, s32[]{:T(128)S(6)} %select_n.157, s32[]{:T(128)} %constant.102.clone.1, s32[]{:T(128)} %constant.102.clone.1) | dynamic-update-slice | bytes 131076 | tf_op jit(solution)/shard_map/dynamic_update_slice | solution.py:137
  67.1 2.0 %dynamic_update_slice.57 = bf16[1,16,4,8192]{3,1,2,0:T(8,128)(2,1)S(1)} dynamic-update-slice(bf16[1,16,4,8192]{3,1,2,0:T(8,128)(2,1)S(1)} %dynamic_update_slice.56, bf16[1,1,4,8192]{3,1,2,0:T(2,128)(2,1)S(1)} %copy.142, s32[]{:T(128)} %constant.102.clone.1, s32[]{:T(128)S(6)} %select_n.159, s32[]{:T(128)} %constant.102.clone.1, s32[]{:T(128)} %constant.102.clone.1) | dynamic-update-slice | bytes 131076 | tf_op jit(solution)/shard_map/dynamic_update_slice | solution.py:128
  69.3 2.0 %dynamic_update_slice.58 = bf16[1,16,4,8192]{3,1,2,0:T(8,128)(2,1)S(1)} dynamic-update-slice(bf16[1,16,4,8192]{3,1,2,0:T(8,128)(2,1)S(1)} %dynamic_update_slice.57, bf16[1,1,4,8192]{3,1,2,0:T(2,128)(2,1)S(1)} %copy.143, s32[]{:T(128)} %constant.102.clone.1, s32[]{:T(128)S(6)} %select_n.161, s32[]{:T(128)} %constant.102.clone.1, s32[]{:T(128)} %constant.102.clone.1) | dynamic-update-slice | bytes 131076 | tf_op jit(solution)/shard_map/dynamic_update_slice | solution.py:137
  71.4 2.0 %dynamic_update_slice.59 = bf16[1,16,4,8192]{3,1,2,0:T(8,128)(2,1)S(1)} dynamic-update-slice(bf16[1,16,4,8192]{3,1,2,0:T(8,128)(2,1)S(1)} %dynamic_update_slice.58, bf16[1,1,4,8192]{3,1,2,0:T(2,128)(2,1)S(1)} %copy.144, s32[]{:T(128)} %constant.102.clone.1, s32[]{:T(128)S(6)} %select_n.163, s32[]{:T(128)} %constant.102.clone.1, s32[]{:T(128)} %constant.102.clone.1) | dynamic-update-slice | bytes 131076 | tf_op jit(solution)/shard_map/dynamic_update_slice | solution.py:128
  73.5 2.0 %dynamic_update_slice.60 = bf16[1,16,4,8192]{3,1,2,0:T(8,128)(2,1)S(1)} dynamic-update-slice(bf16[1,16,4,8192]{3,1,2,0:T(8,128)(2,1)S(1)} %dynamic_update_slice.59, bf16[1,1,4,8192]{3,1,2,0:T(2,128)(2,1)S(1)} %copy.145, s32[]{:T(128)} %constant.102.clone.1, s32[]{:T(128)S(6)} %select_n.165, s32[]{:T(128)} %constant.102.clone.1, s32[]{:T(128)} %constant.102.clone.1) | dynamic-update-slice | bytes 131076 | tf_op jit(solution)/shard_map/dynamic_update_slice | solution.py:137
  75.6 2.0 %dynamic_update_slice.61 = bf16[1,16,4,8192]{3,1,2,0:T(8,128)(2,1)S(1)} dynamic-update-slice(bf16[1,16,4,8192]{3,1,2,0:T(8,128)(2,1)S(1)} %dynamic_update_slice.60, bf16[1,1,4,8192]{3,1,2,0:T(2,128)(2,1)S(1)} %copy.146, s32[]{:T(128)} %constant.102.clone.1, s32[]{:T(128)S(6)} %select_n.167, s32[]{:T(128)} %constant.102.clone.1, s32[]{:T(128)} %constant.102.clone.1) | dynamic-update-slice | bytes 131076 | tf_op jit(solution)/shard_map/dynamic_update_slice | solution.py:128
  77.8 2.0 %dynamic_update_slice.62 = bf16[1,16,4,8192]{3,1,2,0:T(8,128)(2,1)S(1)} dynamic-update-slice(bf16[1,16,4,8192]{3,1,2,0:T(8,128)(2,1)S(1)} %dynamic_update_slice.61, bf16[1,1,4,8192]{3,1,2,0:T(2,128)(2,1)S(1)} %copy.147, s32[]{:T(128)} %constant.102.clone.1, s32[]{:T(128)S(6)} %select_n.169, s32[]{:T(128)} %constant.102.clone.1, s32[]{:T(128)} %constant.102.clone.1) | dynamic-update-slice | bytes 131076 | tf_op jit(solution)/shard_map/dynamic_update_slice | solution.py:137
  79.9 2.0 %dynamic_update_slice.63 = bf16[1,16,4,8192]{3,1,2,0:T(8,128)(2,1)S(1)} dynamic-update-slice(bf16[1,16,4,8192]{3,1,2,0:T(8,128)(2,1)S(1)} %dynamic_update_slice.62, bf16[1,1,4,8192]{3,1,2,0:T(2,128)(2,1)S(1)} %copy.148, s32[]{:T(128)} %constant.102.clone.1, s32[]{:T(128)S(6)} %select_n.171, s32[]{:T(128)} %constant.102.clone.1, s32[]{:T(128)} %constant.102.clone.1) | dynamic-update-slice | bytes 131076 | tf_op jit(solution)/shard_map/dynamic_update_slice | solution.py:128
  81.9 0.3 copy.199
  82.2 1.8 bitcast_reduce_fusion.1
  84.1 2.1 %fusion.7 = f32[16,4,8,8]{3,1,0,2:T(4,128)} fusion(f32[8,16,4,8,128]{4,3,2,1,0:T(8,128)S(1)} %get-tuple-element.23, f32[16,4,8,8]{3,1,0,2:T(4,128)S(1)} %get-tuple-element.22, pred[128]{0:T(512)(128)(4,1)S(1)} %get-tuple-element.25), kind=kLoop, calls=%fused_computation.18 | loop fusion | flops 2617344 | bytes 2130048 | tf_op jit(solution)/shard_map/reduce_sum | solution.py:22
  86.2 1.7 copy.176
  87.9 1.8 fusion.60
  89.7 2.7 %bitcast_reduce_fusion = (f32[16,4,8,8]{3,1,0,2:T(4,128)}, f32[8,16,4,8,128]{4,3,2,1,0:T(8,128)}) fusion(pred[128]{0:T(512)(128)(4,1)S(1)} %get-tuple-element.24, bf16[128,8,128,1,1]{0,2,4,3,1:T(8,128)(2,1)S(1)} %bitcast.176, bf16[16,4,8,8,128]{4,3,2,0,1:T(8,128)(2,1)S(1)} %bitcast.165), kind=kOutput, calls=%fused_computation.6 | convolution fusion | flops 135786496 | bytes 3424384 | tf_op jit(solution)/shard_map/rhlxf,vlf->rhlxv/dot_general | solution.py:38
  92.4 1.1 copy.158
  93.5 2.6 %fusion.9 = f32[16,4,8,8]{3,1,0,2:T(4,128)S(1)} fusion(f32[8,16,4,8,128]{4,3,2,1,0:T(8,128)} %get-tuple-element.21, f32[16,4,8,8]{3,1,0,2:T(4,128)} %get-tuple-element.20, pred[128]{0:T(512)(128)(4,1)S(1)} %get-tuple-element.24), kind=kLoop, calls=%fused_computation.19 | loop fusion | flops 2617344 | bytes 2130048 | tf_op jit(solution)/shard_map/reduce_sum | solution.py:22
  96.5 0.7 reshape.436
  97.2 7.9 %all-to-all-start.1 = ((f32[16,1,256]{2,1,0:T(1,128)}), f32[16,1,256]{2,1,0:T(1,128)S(1)}, u32[]{:S(2)}, u32[]{:S(2)}) async-start(f32[16,1,256]{2,1,0:T(1,128)} %reshape.436), calls=%async_computation.1 | async-start | bytes 32768 | tf_op jit(solution)/shard_map/all_to_all | solution.py:99
  105.3 2.7 %convolution_bitcast_fusion.1 = f32[16,4,8,8,128]{4,3,1,0,2:T(8,128)} fusion(bf16[128,8,128,1,1]{0,2,4,3,1:T(8,128)(2,1)S(1)} %bitcast.181, f32[8,16,4,8,128]{4,3,2,1,0:T(8,128)S(1)} %get-tuple-element.23, f32[16,4,8,8]{3,1,0,2:T(4,128)S(1)} %get-tuple-element.22, pred[128]{0:T(512)(128)(4,1)S(1)} %get-tuple-element.25), kind=kOutput, calls=%fused_computation.17 | convolution fusion | flops 807403520 | bytes 4472960 | tf_op jit(solution)/shard_map/urpyj,jpi->urpyi/dot_general | solution.py:23
  108.0 2.7 %convolution_bitcast_fusion = f32[16,4,8,8,128]{4,3,1,0,2:T(8,128)} fusion(bf16[128,8,128,1,1]{0,2,4,3,1:T(8,128)(2,1)S(1)} %bitcast.182, f32[8,16,4,8,128]{4,3,2,1,0:T(8,128)S(1)} %copy-done, f32[16,4,8,8]{3,1,0,2:T(4,128)S(1)} %copy-done.1, pred[128]{0:T(512)(128)(4,1)S(1)} %get-tuple-element.24), kind=kOutput, calls=%fused_computation.16 | convolution fusion | flops 807403520 | bytes 4472960 | tf_op jit(solution)/shard_map/urpyj,jpi->urpyi/dot_general | solution.py:23
  110.9 0.7 reshape.438
  111.6 0.8 all-to-all-done.1
  112.4 6.6 %all-to-all-start.2 = ((f32[16,1,256]{2,1,0:T(1,128)}), f32[16,1,256]{2,1,0:T(1,128)S(1)}, u32[]{:S(2)}, u32[]{:S(2)}) async-start(f32[16,1,256]{2,1,0:T(1,128)} %reshape.438), calls=%async_computation.2 | async-start | bytes 32768 | tf_op jit(solution)/shard_map/all_to_all | solution.py:100
  119.0 3.5 %fusion.2 = f32[1,16,4,64,128]{4,3,2,0,1:T(8,128)} fusion(f32[16,4,8,8,128]{4,3,1,0,2:T(8,128)} %convolution_bitcast_fusion, f32[16,4,8,8,128]{4,3,1,0,2:T(8,128)S(1)} %copy-done.2, f32[16,4,64]{2,1,0:T(4,128)S(1)} %copy.166, f32[16,4,64]{2,1,0:T(4,128)S(1)} %copy.162), kind=kLoop, calls=%fused_computation.4 | loop fusion | flops 1572864 | bytes 6324224 | tf_op jit(solution)/shard_map/add | solution.py:80
  122.5 3.8 %all-to-all-done.2 = f32[16,1,256]{2,1,0:T(1,128)S(1)} async-done(((f32[16,1,256]{2,1,0:T(1,128)}), f32[16,1,256]{2,1,0:T(1,128)S(1)}, u32[]{:S(2)}, u32[]{:S(2)}) %all-to-all-start.2) | async-done | bytes 16416 | tf_op jit(solution)/shard_map/all_to_all | solution.py:100
  126.4 3.9 %all-to-all-start = ((f32[1,16,4,64,128]{4,3,2,0,1:T(8,128)}), f32[1,16,4,64,128]{4,3,2,0,1:T(8,128)S(1)}, u32[]{:S(2)}, u32[]{:S(2)}) async-start(f32[1,16,4,64,128]{4,3,2,0,1:T(8,128)} %fusion.2), calls=%async_computation | async-start | bytes 4194304 | tf_op jit(solution)/shard_map/all_to_all | solution.py:98
  130.9 12.8 %fusion.13 = (bf16[260,1024]{1,0:T(8,128)(2,1)S(1)}, bf16[260,1024]{1,0:T(8,128)(2,1)S(1)}) fusion(bf16[1,4,2,1024]{3,2,1,0:T(2,128)(2,1)S(1)} %bitcast.186, bf16[1,256,2,1024]{3,2,1,0:T(2,128)(2,1)} %bitcast.174), kind=kLoop, calls=%fused_computation.26 | loop fusion | flops 2129920 | bytes 2129920 | tf_op jit(solution)/shard_map/slice | solution.py:53
  143.9 0.4 fusion.61
  144.3 0.2 fusion.33
  144.9 0.5 convolution_bitcast_fusion.2
  145.4 0.5 broadcast.118
  146.0 0.7 reduce.10
  146.7 0.7 reduce.11
  147.6 31.6 %all-to-all-done = f32[1,16,4,64,128]{4,3,2,0,1:T(8,128)S(1)} async-done(((f32[1,16,4,64,128]{4,3,2,0,1:T(8,128)}), f32[1,16,4,64,128]{4,3,2,0,1:T(8,128)S(1)}, u32[]{:S(2)}, u32[]{:S(2)}) %all-to-all-start) | async-done | bytes 2097184 | tf_op jit(solution)/shard_map/all_to_all | solution.py:98
  179.2 0.7 fusion
  180.2 0.2 fusion.40
  180.5 0.7 copy.180
  (87 shorter events, 4.1 us)
Async XLA Ops:
  0.0 43.7 %copy-start.6 = (bf16[1,1,4,8192]{3,2,1,0:T(4,128)(2,1)S(1)}, bf16[1,1,4,8192]{3,2,1,0:T(4,128)(2,1)}, u32[]{:S(2)}) copy-start(bf16[1,1,4,8192]{3,2,1,0:T(4,128)(2,1)} %param.7) | copy-start | bytes 196612
  0.0 44.0 %copy-start.9 = (s32[32]{0:T(128)S(1)}, s32[32]{0:T(128)}, u32[]{:S(2)}) copy-start(s32[32]{0:T(128)} %param.13) | copy-start | bytes 388
  0.0 7.8 %collective-permute-start = (bf16[1,1,4,8192]{3,2,1,0:T(4,128)(2,1)}, bf16[1,1,4,8192]{3,2,1,0:T(4,128)(2,1)S(1)}, u32[]{:S(2)}, u32[]{:S(2)}) collective-permute-start(bf16[1,1,4,8192]{3,2,1,0:T(4,128)(2,1)} %param.7), channel_id=1, source_target_pairs={{0,1},{1,2},{2,3},{3,4},{4,5},{5,6},{6,7},{7,8},{8,9},{9,10},{10,1... | collective-permute-start | bytes 196616 | tf_op jit(solution)/shard_map/ppermute | solution.py:125
  3.5 4.5 %collective-permute-start.1 = (bf16[1,1,4,8192]{3,2,1,0:T(4,128)(2,1)}, bf16[1,1,4,8192]{3,2,1,0:T(4,128)(2,1)S(1)}, u32[]{:S(2)}, u32[]{:S(2)}) collective-permute-start(bf16[1,1,4,8192]{3,2,1,0:T(4,128)(2,1)} %param.7), channel_id=1, source_target_pairs={{0,15},{1,0},{2,1},{3,2},{4,3},{5,4},{6,5},{7,6},{8,7},{9,8},{10,9... | collective-permute-start | bytes 196616 | tf_op jit(solution)/shard_map/ppermute | solution.py:132
  7.8 5.1 %collective-permute-start.2 = (bf16[1,1,4,8192]{3,2,1,0:T(4,128)(2,1)S(1)}, bf16[1,1,4,8192]{3,2,1,0:T(4,128)(2,1)S(1)}, u32[]{:S(2)}, u32[]{:S(2)}) collective-permute-start(bf16[1,1,4,8192]{3,2,1,0:T(4,128)(2,1)S(1)} %collective-permute-done), channel_id=1, source_target_pairs={{0,1},{1,2},{2,3},{3,4},{4,5},{5,6},{6,7},{7,8},{8,9},{9,10},{10,1... | collective-permute-start | bytes 196616 | tf_op jit(solution)/shard_map/ppermute | solution.py:125
  8.0 5.1 %collective-permute-start.3 = (bf16[1,1,4,8192]{3,2,1,0:T(4,128)(2,1)S(1)}, bf16[1,1,4,8192]{3,2,1,0:T(4,128)(2,1)S(1)}, u32[]{:S(2)}, u32[]{:S(2)}) collective-permute-start(bf16[1,1,4,8192]{3,2,1,0:T(4,128)(2,1)S(1)} %collective-permute-done.1), channel_id=1, source_target_pairs={{0,15},{1,0},{2,1},{3,2},{4,3},{5,4},{6,5},{7,6},{8,7},{9,8},{10,9... | collective-permute-start | bytes 196616 | tf_op jit(solution)/shard_map/ppermute | solution.py:132
  13.0 4.9 %collective-permute-start.4 = (bf16[1,1,4,8192]{3,2,1,0:T(4,128)(2,1)S(1)}, bf16[1,1,4,8192]{3,2,1,0:T(4,128)(2,1)S(1)}, u32[]{:S(2)}, u32[]{:S(2)}) collective-permute-start(bf16[1,1,4,8192]{3,2,1,0:T(4,128)(2,1)S(1)} %collective-permute-done.2), channel_id=1, source_target_pairs={{0,1},{1,2},{2,3},{3,4},{4,5},{5,6},{6,7},{7,8},{8,9},{9,10},{10,1... | collective-permute-start | bytes 196616 | tf_op jit(solution)/shard_map/ppermute | solution.py:125
  13.1 4.9 %collective-permute-start.5 = (bf16[1,1,4,8192]{3,2,1,0:T(4,128)(2,1)S(1)}, bf16[1,1,4,8192]{3,2,1,0:T(4,128)(2,1)S(1)}, u32[]{:S(2)}, u32[]{:S(2)}) collective-permute-start(bf16[1,1,4,8192]{3,2,1,0:T(4,128)(2,1)S(1)} %collective-permute-done.3), channel_id=1, source_target_pairs={{0,15},{1,0},{2,1},{3,2},{4,3},{5,4},{6,5},{7,6},{8,7},{9,8},{10,9... | collective-permute-start | bytes 196616 | tf_op jit(solution)/shard_map/ppermute | solution.py:132
  17.9 4.9 %collective-permute-start.6 = (bf16[1,1,4,8192]{3,2,1,0:T(4,128)(2,1)S(1)}, bf16[1,1,4,8192]{3,2,1,0:T(4,128)(2,1)S(1)}, u32[]{:S(2)}, u32[]{:S(2)}) collective-permute-start(bf16[1,1,4,8192]{3,2,1,0:T(4,128)(2,1)S(1)} %collective-permute-done.4), channel_id=1, source_target_pairs={{0,1},{1,2},{2,3},{3,4},{4,5},{5,6},{6,7},{7,8},{8,9},{9,10},{10,1... | collective-permute-start | bytes 196616 | tf_op jit(solution)/shard_map/ppermute | solution.py:125
  18.0 4.9 %collective-permute-start.7 = (bf16[1,1,4,8192]{3,2,1,0:T(4,128)(2,1)S(1)}, bf16[1,1,4,8192]{3,2,1,0:T(4,128)(2,1)S(1)}, u32[]{:S(2)}, u32[]{:S(2)}) collective-permute-start(bf16[1,1,4,8192]{3,2,1,0:T(4,128)(2,1)S(1)} %collective-permute-done.5), channel_id=1, source_target_pairs={{0,15},{1,0},{2,1},{3,2},{4,3},{5,4},{6,5},{7,6},{8,7},{9,8},{10,9... | collective-permute-start | bytes 196616 | tf_op jit(solution)/shard_map/ppermute | solution.py:132
  22.8 4.9 %collective-permute-start.8 = (bf16[1,1,4,8192]{3,2,1,0:T(4,128)(2,1)S(1)}, bf16[1,1,4,8192]{3,2,1,0:T(4,128)(2,1)S(1)}, u32[]{:S(2)}, u32[]{:S(2)}) collective-permute-start(bf16[1,1,4,8192]{3,2,1,0:T(4,128)(2,1)S(1)} %collective-permute-done.6), channel_id=1, source_target_pairs={{0,1},{1,2},{2,3},{3,4},{4,5},{5,6},{6,7},{7,8},{8,9},{9,10},{10,1... | collective-permute-start | bytes 196616 | tf_op jit(solution)/shard_map/ppermute | solution.py:125
  22.9 15.4 %collective-permute-start.9 = (bf16[1,1,4,8192]{3,2,1,0:T(4,128)(2,1)S(1)}, bf16[1,1,4,8192]{3,2,1,0:T(4,128)(2,1)S(1)}, u32[]{:S(2)}, u32[]{:S(2)}) collective-permute-start(bf16[1,1,4,8192]{3,2,1,0:T(4,128)(2,1)S(1)} %collective-permute-done.7), channel_id=1, source_target_pairs={{0,15},{1,0},{2,1},{3,2},{4,3},{5,4},{6,5},{7,6},{8,7},{9,8},{10,9... | collective-permute-start | bytes 196616 | tf_op jit(solution)/shard_map/ppermute | solution.py:132
  27.7 15.1 %collective-permute-start.10 = (bf16[1,1,4,8192]{3,2,1,0:T(4,128)(2,1)S(1)}, bf16[1,1,4,8192]{3,2,1,0:T(4,128)(2,1)S(1)}, u32[]{:S(2)}, u32[]{:S(2)}) collective-permute-start(bf16[1,1,4,8192]{3,2,1,0:T(4,128)(2,1)S(1)} %collective-permute-done.8), channel_id=1, source_target_pairs={{0,1},{1,2},{2,3},{3,4},{4,5},{5,6},{6,7},{7,8},{8,9},{9,10},{10,1... | collective-permute-start | bytes 196616 | tf_op jit(solution)/shard_map/ppermute | solution.py:125
  29.7 58.2 %collective-permute-start.15 = (bf16[1,128,2,1024]{1,3,2,0:T(8,128)(2,1)}, bf16[1,128,2,1024]{1,3,2,0:T(8,128)(2,1)}, u32[]{:S(2)}, u32[]{:S(2)}) collective-permute-start(bf16[1,128,2,1024]{1,3,2,0:T(8,128)(2,1)} %copy.155), channel_id=1, source_target_pairs={{0,496},{16,0},{32,16},{48,32},{64,48},{80,64},{96,80},{112,96},{1... | collective-permute-start | bytes 1572872 | tf_op jit(solution)/shard_map/ppermute | solution.py:15
  38.4 8.4 %collective-permute-start.11 = (bf16[1,1,4,8192]{3,2,1,0:T(4,128)(2,1)S(1)}, bf16[1,1,4,8192]{3,2,1,0:T(4,128)(2,1)S(1)}, u32[]{:S(2)}, u32[]{:S(2)}) collective-permute-start(bf16[1,1,4,8192]{3,2,1,0:T(4,128)(2,1)S(1)} %collective-permute-done.9), channel_id=1, source_target_pairs={{0,15},{1,0},{2,1},{3,2},{4,3},{5,4},{6,5},{7,6},{8,7},{9,8},{10,9... | collective-permute-start | bytes 196616 | tf_op jit(solution)/shard_map/ppermute | solution.py:132
  42.8 6.6 %collective-permute-start.12 = (bf16[1,1,4,8192]{3,2,1,0:T(4,128)(2,1)S(1)}, bf16[1,1,4,8192]{3,2,1,0:T(4,128)(2,1)S(1)}, u32[]{:S(2)}, u32[]{:S(2)}) collective-permute-start(bf16[1,1,4,8192]{3,2,1,0:T(4,128)(2,1)S(1)} %collective-permute-done.10), channel_id=1, source_target_pairs={{0,1},{1,2},{2,3},{3,4},{4,5},{5,6},{6,7},{7,8},{8,9},{9,10},{10,1... | collective-permute-start | bytes 196616 | tf_op jit(solution)/shard_map/ppermute | solution.py:125
  46.7 30.9 %collective-permute-start.13 = (bf16[1,1,4,8192]{3,2,1,0:T(4,128)(2,1)S(1)}, bf16[1,1,4,8192]{3,2,1,0:T(4,128)(2,1)S(1)}, u32[]{:S(2)}, u32[]{:S(2)}) collective-permute-start(bf16[1,1,4,8192]{3,2,1,0:T(4,128)(2,1)S(1)} %collective-permute-done.11), channel_id=1, source_target_pairs={{0,15},{1,0},{2,1},{3,2},{4,3},{5,4},{6,5},{7,6},{8,7},{9,8},{10,9... | collective-permute-start | bytes 196616 | tf_op jit(solution)/shard_map/ppermute | solution.py:132
  49.4 30.3 %collective-permute-start.14 = (bf16[1,1,4,8192]{3,2,1,0:T(4,128)(2,1)S(1)}, bf16[1,1,4,8192]{3,2,1,0:T(4,128)(2,1)S(1)}, u32[]{:S(2)}, u32[]{:S(2)}) collective-permute-start(bf16[1,1,4,8192]{3,2,1,0:T(4,128)(2,1)S(1)} %collective-permute-done.12), channel_id=1, source_target_pairs={{0,1},{1,2},{2,3},{3,4},{4,5},{5,6},{6,7},{7,8},{8,9},{9,10},{10,1... | collective-permute-start | bytes 196616 | tf_op jit(solution)/shard_map/ppermute | solution.py:125
  92.4 3.9 %copy-start.3 = (f32[16,4,8,8]{0,3,2,1:T(8,128)S(1)}, f32[16,4,8,8]{0,3,2,1:T(8,128)}, u32[]{:S(2)}) copy-start(f32[16,4,8,8]{0,3,2,1:T(8,128)} %copy.176) | copy-start | bytes 49156
  93.5 11.7 %copy-start.4 = (bf16[128,1,1024]{0,2,1:T(8,128)(2,1)S(1)}, bf16[128,1,1024]{0,2,1:T(8,128)(2,1)}, u32[]{:S(2)}) copy-start(bf16[128,1,1024]{0,2,1:T(8,128)(2,1)} %get-tuple-element.10) | copy-start | bytes 786436
  97.2 15.3 %all-to-all-start.1 = ((f32[16,1,256]{2,1,0:T(1,128)}), f32[16,1,256]{2,1,0:T(1,128)S(1)}, u32[]{:S(2)}, u32[]{:S(2)}) async-start(f32[16,1,256]{2,1,0:T(1,128)} %reshape.436), calls=%async_computation.1 | async-start | bytes 32768 | tf_op jit(solution)/shard_map/all_to_all | solution.py:99
  105.3 2.8 %copy-start = (f32[8,16,4,8,128]{4,3,2,1,0:T(8,128)S(1)}, f32[8,16,4,8,128]{4,3,2,1,0:T(8,128)}, u32[]{:S(2)}) copy-start(f32[8,16,4,8,128]{4,3,2,1,0:T(8,128)} %get-tuple-element.21) | copy-start | bytes 6291460
  105.3 2.8 %copy-start.1 = (f32[16,4,8,8]{3,1,0,2:T(4,128)S(1)}, f32[16,4,8,8]{3,1,0,2:T(4,128)}, u32[]{:S(2)}) copy-start(f32[16,4,8,8]{3,1,0,2:T(4,128)} %get-tuple-element.20) | copy-start | bytes 49156
  105.3 2.7 %copy-start.5 = (bf16[128,1,1024]{0,2,1:T(8,128)(2,1)S(1)}, bf16[128,1,1024]{0,2,1:T(8,128)(2,1)}, u32[]{:S(2)}) copy-start(bf16[128,1,1024]{0,2,1:T(8,128)(2,1)} %get-tuple-element.12) | copy-start | bytes 786436
  108.0 11.0 %copy-start.2 = (f32[16,4,8,8,128]{4,3,1,0,2:T(8,128)S(1)}, f32[16,4,8,8,128]{4,3,1,0,2:T(8,128)}, u32[]{:S(2)}) copy-start(f32[16,4,8,8,128]{4,3,1,0,2:T(8,128)} %convolution_bitcast_fusion.1) | copy-start | bytes 6291460
  112.4 13.9 %all-to-all-start.2 = ((f32[16,1,256]{2,1,0:T(1,128)}), f32[16,1,256]{2,1,0:T(1,128)S(1)}, u32[]{:S(2)}, u32[]{:S(2)}) async-start(f32[16,1,256]{2,1,0:T(1,128)} %reshape.438), calls=%async_computation.2 | async-start | bytes 32768 | tf_op jit(solution)/shard_map/all_to_all | solution.py:100
  122.5 8.4 %copy-start.8 = (bf16[1,1,4,2,1024]{4,3,2,1,0:T(2,128)(2,1)S(1)}, bf16[1,1,4,2,1024]{4,3,2,1,0:T(2,128)(2,1)}, u32[]{:S(2)}) copy-start(bf16[1,1,4,2,1024]{4,3,2,1,0:T(2,128)(2,1)} %param.8) | copy-start | bytes 49156
  126.4 52.9 %all-to-all-start = ((f32[1,16,4,64,128]{4,3,2,0,1:T(8,128)}), f32[1,16,4,64,128]{4,3,2,0,1:T(8,128)S(1)}, u32[]{:S(2)}, u32[]{:S(2)}) async-start(f32[1,16,4,64,128]{4,3,2,0,1:T(8,128)} %fusion.2), calls=%async_computation | async-start | bytes 4194304 | tf_op jit(solution)/shard_map/all_to_all | solution.py:98
  130.9 13.0 %copy-start.7 = (bf16[1,1,4,8192]{3,2,1,0:T(4,128)(2,1)S(1)}, bf16[1,1,4,8192]{3,2,1,0:T(4,128)(2,1)}, u32[]{:S(2)}) copy-start(bf16[1,1,4,8192]{3,2,1,0:T(4,128)(2,1)} %param.7) | copy-start | bytes 196612
